TPU v7x, 512 devices: a whole 4x8x8 slice. The times are simulated.
512 devices in a mesh: segment: 16 (over z, core), mp: 32 (over y, x).
Axes of the slice: x: 4, y: 8, z: 8, core: 2. Of those that a mesh axis runs over, the one named last changes fastest.
Arguments:
- rows: bfloat16 [16, 2, 128, 8192], P('segment', None, None, 'mp'), may hold values from -6 to 6
- carry: bfloat16 [16, 128, 8192], P('segment', None, 'mp'), may hold values from -6 to 6
- weights: bfloat16 [16, 2, 8192, 4096], P('segment', None, None, 'mp'), may hold values from -1.1932427 to 1.1932427
- neighbours: int32 [16, 2, 2, 2], P('segment'), may hold values from 0 to 7, all different within a row
Outputs:
- passed: bfloat16 [16, 128, 8192], P('segment', None, 'mp')
- returned: bfloat16 [16, 128, 8192], P('segment', None, 'mp')
- kv_grad: bfloat16 [1024, 2, 4096], P(None, None, 'mp')
Inputs may be any that keep to these rules, and one draw needn't show every extreme that they name: Each group's 2 neighbours are different pool blocks; pool blocks are numbered by encoder segment in order, then by row.
All inputs are finite; a program needn't handle non-finite values.
Results may differ from a plain program's by a relative error of at most 0.02.
The roundings to bfloat16 on the way count: a program that leaves them out, or rounds other values in their place, can miss the bound.
Values may be sent and summed in bfloat16 or wider, within the bound.
No kernel may reach another device: no remote copies, remote signals or barrier semaphores. Data moves between devices by JAX's collectives and lax.ppermute only.
A program may use at most 64 MiB of HBM per device.

v0:
```python
import functools
import math
import numpy as np
import jax
import jax.numpy as jnp
from jax import lax
from jax.sharding import Mesh, PartitionSpec as P

GROUP = 64
NBLEN = 128
NEIGH = 2


def from_behind(x, axis, by):
    devices = lax.axis_size(axis)
    return lax.ppermute(x, axis, [(i, (i + by) % devices) for i in range(devices)])


def attend(queries, key_rows, score_scale):
    scores = (
        jnp.einsum("cqd,ckd->cqk", queries, key_rows, preferred_element_type=jnp.float32)
        * score_scale
    )
    soft = jax.nn.softmax(scores, axis=-1)
    return (soft, soft.astype(jnp.bfloat16))


def attend_back(queries, key_rows, value_rows, soft, rounded, upstream, score_scale):
    d_soft = jnp.einsum("cqd,ckd->cqk", upstream, value_rows, preferred_element_type=jnp.float32)
    grad_values = jnp.einsum("cqk,cqd->ckd", rounded, upstream, preferred_element_type=jnp.float32)
    d_scores = soft * (d_soft - jnp.sum(d_soft * soft, axis=-1, keepdims=True))
    grad_queries = (
        jnp.einsum("cqk,ckd->cqd", d_scores, key_rows.astype(jnp.float32)) * score_scale
    ).astype(jnp.bfloat16)
    grad_keys = jnp.einsum("cqk,cqd->ckd", d_scores, queries.astype(jnp.float32)) * score_scale
    return (grad_queries, grad_keys, grad_values)


def head_sum(terms, axis, tie):
    count, width, tokens = terms.shape
    rounded = terms.astype(jnp.bfloat16)
    if isinstance(axis, tuple):
        tall, wide = (lax.axis_size(axis[0]), lax.axis_size(axis[1]))
        parts = rounded.reshape(count, tall, wide, width // (tall * wide), tokens).transpose(
            1, 2, 0, 3, 4
        )
        partial = lax.psum_scatter(parts, axis[0], scatter_dimension=0, tiled=True)[0]
        partial, tie = lax.optimization_barrier((partial, tie))
        moved = lax.all_to_all(partial, axis[1], 0, 0, tiled=True)
        summed = jnp.sum(moved.astype(jnp.float32), axis=0)
    else:
        devices = lax.axis_size(axis)
        parts = rounded.reshape(count, devices, width // devices, tokens).transpose(1, 0, 2, 3)
        moved = lax.all_to_all(parts, axis, 0, 0, tiled=True)
        summed = jnp.sum(moved.astype(jnp.float32), axis=0)
    return (summed.transpose(0, 2, 1), tie)


def segment_sum(contrib, axis):
    devices = lax.axis_size(axis)
    parts = contrib.reshape(devices, contrib.shape[0] // devices, contrib.shape[1])
    moved = lax.all_to_all(parts, axis, 0, 0, tiled=True)
    summed = jnp.sum(moved.astype(jnp.float32), axis=0).astype(jnp.bfloat16)
    spread = jnp.broadcast_to(summed[None], (devices,) + summed.shape)
    return lax.all_to_all(spread, axis, 0, 0, tiled=True).reshape(contrib.shape)


def per_device(mp, stages, rows, carry, weights, neighbours):
    seg = ("sg", "sr")
    segments = lax.axis_size(seg)
    encoders = lax.axis_size("sr")
    first_encoder = segments - encoders
    last_group = lax.axis_size("sg") - 1
    group = lax.axis_index("sg")
    is_encoder = group == last_group
    local_rows = rows[0]
    local_carry = carry[0]
    gathered = jnp.concatenate([local_rows, local_carry[None]], axis=0)
    for stage in stages:
        gathered = lax.all_gather(gathered, stage, axis=2, tiled=True)
    full_rows, full_carry = (gathered[:2], gathered[2])
    tokens = local_rows.shape[1]
    width = full_rows.shape[2]
    head = weights.shape[3]
    w_query = weights[0, 0]
    w_out = weights[0, 1]

    def encode():
        flat = full_rows.reshape(2 * tokens, width)
        keyval = jnp.concatenate(
            [
                jnp.dot(flat, w_query, preferred_element_type=jnp.float32),
                jnp.dot(flat, w_out, preferred_element_type=jnp.float32),
            ],
            axis=-1,
        ).astype(jnp.bfloat16)
        return (keyval, jnp.zeros((2 * tokens, head), jnp.bfloat16))

    def decode():
        queries = jnp.dot(
            full_rows.reshape(2 * tokens, width), w_query, preferred_element_type=jnp.float32
        ).astype(jnp.bfloat16)
        return (jnp.zeros((2 * tokens, 2 * head), jnp.bfloat16), queries)

    encoded, queries = lax.cond(is_encoder, encode, decode)
    per_encoder = 2 * tokens // NBLEN
    pool_blocks = encoders * per_encoder
    piece = encoded
    for target in range(last_group):
        arrived = lax.ppermute(encoded, "sg", [(last_group, target)])
        piece = jnp.where(group == target, arrived, piece)
    pool = lax.all_gather(piece, "sr", axis=0, tiled=True).reshape(pool_blocks, NBLEN, 2 * head)
    groups = tokens // GROUP
    local_nbr = neighbours[0]
    score_scale = 1.0 / math.sqrt(head)
    query_blocks = queries.reshape(2, groups, GROUP, head)

    def fetch(batch):
        picked = pool[local_nbr[batch]].reshape(groups, NEIGH * NBLEN, 2 * head)
        return (picked[..., :head], picked[..., head:])

    keys_fwd, values_fwd = fetch(0)
    soft_fwd, rounded_fwd = attend(query_blocks[0], keys_fwd, score_scale)
    mixed = jnp.einsum(
        "cqk,ckd->cqd", rounded_fwd, values_fwd, preferred_element_type=jnp.float32
    ).astype(jnp.bfloat16)
    mixed_flat = mixed.reshape(tokens, head)
    upstream = (
        jnp.dot(full_carry, w_out, preferred_element_type=jnp.float32)
        .astype(jnp.bfloat16)
        .reshape(groups, GROUP, head)
    )
    keys_back, values_back = fetch(1)
    soft_back, rounded_back = attend(query_blocks[1], keys_back, score_scale)
    grad_queries, grad_keys, grad_values = attend_back(
        query_blocks[1], keys_back, values_back, soft_back, rounded_back, upstream, score_scale
    )
    grad_flat = grad_queries.reshape(tokens, head)
    terms = jnp.stack(
        [
            lax.dot_general(
                w_out, mixed_flat, (((1,), (1,)), ((), ())), preferred_element_type=jnp.float32
            ),
            lax.dot_general(
                w_query, grad_flat, (((1,), (1,)), ((), ())), preferred_element_type=jnp.float32
            ),
        ]
    )
    onehot = (
        local_nbr[1][..., None] == jnp.arange(pool_blocks, dtype=jnp.int32)[None, None, :]
    ).astype(jnp.float32)
    grad_keyval = jnp.concatenate([grad_keys, grad_values], axis=-1).reshape(
        groups, NEIGH, NBLEN, 2 * head
    )
    contrib = jnp.einsum("cbp,cbrf->prf", onehot, grad_keyval)
    contrib = jnp.where(is_encoder, jnp.zeros_like(contrib), contrib)
    pooled = segment_sum(contrib.astype(jnp.bfloat16).reshape(pool_blocks * NBLEN, 2 * head), seg)
    kv_grad = pooled.reshape(pool_blocks * NBLEN, 2, head)
    summed, kv_grad = head_sum(terms, mp, kv_grad)
    out_sum, grad_input = summed
    forward_rows = (local_rows[0].astype(jnp.float32) + out_sum).astype(jnp.bfloat16)
    forward_rows = jnp.where(is_encoder, local_carry, forward_rows)
    passed = from_behind(forward_rows[None], seg, 1)
    back = local_carry.astype(jnp.float32) + grad_input
    back_rows = jnp.where(is_encoder, local_carry, back.astype(jnp.bfloat16))
    returned = from_behind(back_rows[None], seg, -1)
    return (passed, returned, kv_grad)


def split_mesh(mesh):
    devices = mesh.devices
    segments = devices.shape[0]
    encoders = segments // 4
    groups = segments // encoders
    try:
        xs = [d.coords[0] for d in devices[0]]
        ys = [d.coords[1] for d in devices[0]]
        wide = len(set(xs))
        tall = devices.shape[1] // wide
        grid_x = np.array(xs).reshape(tall, wide)
        grid_y = np.array(ys).reshape(tall, wide)
        ok = (
            wide * tall == devices.shape[1]
            and wide > 1
            and (tall > 1)
            and (grid_x == grid_x[:1]).all()
            and (grid_y == grid_y[:, :1]).all()
        )
    except (AttributeError, TypeError, IndexError, ValueError):
        ok = False
    if ok:
        view = devices.reshape(groups, encoders, tall, wide)
        return (Mesh(view, ("sg", "sr", "my", "mx")), ("my", "mx"), ("mx", "my"))
    view = devices.reshape(groups, encoders, devices.shape[1])
    return (Mesh(view, ("sg", "sr", "mp")), "mp", ("mp",))


def solution(mesh):
    inner, mp, stages = split_mesh(mesh)
    seg = ("sg", "sr")
    placed = (
        P(seg, None, None, mp),
        P(seg, None, mp),
        P(seg, None, None, mp),
        P(seg, None, None, None),
    )
    return jax.shard_map(
        functools.partial(per_device, mp, stages),
        mesh=inner,
        in_specs=placed,
        out_specs=(P(seg, None, mp), P(seg, None, mp), P(None, None, mp)),
        check_vma=False,
    )
```

profile of v0, /device:TPU:24, one launch (start us, length us, event | category | flops | bytes accessed | tf_op | source)
XLA Modules:
  0.0 234.3 jit_solution(7432874130987226434)
XLA Ops:
  7.2 0.0 copy-start.3
  7.2 0.0 all-gather.2.cloned.1.call-start
  7.2 1.0 pad_maximum_fusion.2
  8.2 14.4 %all_gather.9 = bf16[3,128,1024]{2,1,0:T(8,128)(2,1)} all-gather(bf16[3,128,256]{2,1,0:T(8,128)(2,1)S(1)} %pad_maximum_fusion.2), channel_id=1, replica_groups=mesh['sg'=4,'sr'=4,'my'=8,'mx'=4] {'mx'}, dimensions={2}, use_global_device_ids=true | all-gather | bytes 983040 | tf_op jit(solution)/shard_map/all_gather | solution.py:80
  22.6 0.0 all-gather.2.cloned.1.call-update
  22.6 0.0 reduce-scatter.2.cloned.1.call-start
  22.7 0.0 copy-done.3
  22.7 0.1 reshape.139
  22.8 0.1 reshape.147
  22.9 3.8 %slice_bitcast_fusion.2 = (bf16[8192,128]{1,0:T(8,128)(2,1)}, bf16[8192,128]{1,0:T(8,128)(2,1)S(1)}) fusion(bf16[1,2,8192,128]{3,2,1,0:T(8,128)(2,1)} %param.8), kind=kLoop, calls=%fused_computation.15 | loop fusion | bytes 8388608 | tf_op jit(solution)/shard_map/squeeze | solution.py:86
  26.7 77.2 %all-gather.2.cloned.1.call-done = bf16[3,128,8192]{2,1,0:T(8,128)(2,1)} async-done(((bf16[3,128,1024]{2,1,0:T(8,128)(2,1)}), bf16[3,128,8192]{2,1,0:T(8,128)(2,1)}) %all-gather.2.cloned.1.call-update) | async-done | bytes 6291472 | tf_op jit(solution)/shard_map/all_gather | solution.py:80
  103.9 0.0 slice-start
  103.9 0.0 copy-start
  103.9 2.2 slice-done
  106.1 0.7 copy-done
  106.7 1.3 conditional.1
  106.7 1.3 convolution_convert_fusion
  108.1 1.3 collective-permute-start.2
  109.4 0.7 collective-permute-start.1
  110.1 0.7 collective-permute-start
  110.7 2.9 %fusion.12 = bf16[128,128]{1,0:T(8,128)(2,1)S(1)} fusion(bf16[3,128,8192]{2,1,0:T(8,128)(2,1)} %all-gather.2.cloned.1.call-done, bf16[1,2,8192,128]{3,2,1,0:T(8,128)(2,1)} %param.8), kind=kOutput, calls=%fused_computation.29 | convolution fusion | flops 268451840 | bytes 4227072 | tf_op jit(solution)/shard_map/dot_general | solution.py:129
  113.7 6.7 %collective-permute-done.2 = bf16[256,256]{1,0:T(8,128)(2,1)S(1)} collective-permute-done((bf16[256,256]{1,0:T(8,128)(2,1)S(1)}, bf16[256,256]{1,0:T(8,128)(2,1)S(1)}, u32[]{:S(2)}, u32[]{:S(2)}) %collective-permute-start.2) | collective-permute-done | bytes 131104 | tf_op jit(solution)/shard_map/ppermute | solution.py:110
  120.4 0.0 collective-permute-done.1
  120.4 0.0 collective-permute-done
  120.4 11.1 %all_gather.11 = bf16[1024,256]{1,0:T(8,128)(2,1)S(1)} all-gather(bf16[256,256]{1,0:T(8,128)(2,1)S(1)} %select_select_fusion), channel_id=1, replica_groups=mesh['sg'=4,'sr'=4,'my'=8,'mx'=4] {'sr'}, dimensions={0}, use_global_device_ids=true | all-gather | bytes 655360 | tf_op jit(solution)/shard_map/all_gather | solution.py:112
  131.5 0.6 gather_fusion.1
  132.1 0.6 gather_fusion
  132.7 0.2 convolution_multiply_fusion.2
  132.8 0.2 fusion.33
  133.0 0.3 convolution_convert_fusion.5
  133.3 0.2 convolution_multiply_fusion.1
  133.5 0.4 fusion.32
  133.9 0.3 multiply_reduce_fusion
  134.1 0.3 fusion.11
  134.5 2.3 fusion.3
  136.8 2.5 %copy.23 = bf16[8192,128]{1,0:T(8,128)(2,1)} copy(bf16[8192,128]{0,1:T(8,128)(2,1)S(1)} %fusion.3) | data formatting | bytes 4194304 | tf_op jit(solution)/shard_map/stack | solution.py:139
  139.3 2.3 fusion.2
  141.6 2.5 %copy.22 = bf16[8192,128]{1,0:T(8,128)(2,1)} copy(bf16[8192,128]{0,1:T(8,128)(2,1)S(1)} %fusion.2) | data formatting | bytes 4194304 | tf_op jit(solution)/shard_map/stack | solution.py:139
  144.0 4.5 %maximum_bitcast_fusion = bf16[8,4,2,256,128]{4,3,2,1,0:T(8,128)(2,1)} fusion(bf16[1,8,4,256,128]{4,3,0,2,1:T(8,128)(2,1)} %bitcast.82, bf16[1,8,4,256,128]{4,3,0,2,1:T(8,128)(2,1)} %bitcast.83), kind=kLoop, calls=%fused_computation.12 | loop fusion | flops 2097152 | bytes 8388608 | tf_op jit(solution)/shard_map/transpose | solution.py:44
  148.6 0.0 reduce-scatter.2.cloned.1.call-update
  148.6 0.1 copy.17
  148.7 0.3 fusion.23
  149.0 0.4 convolution_multiply_fusion
  149.4 0.1 reshape.135
  149.5 0.5 copy.18
  150.0 0.5 fusion.6
  150.5 0.1 copy.19
  150.6 21.9 %all_to_all.15 = bf16[16,64,256]{2,1,0:T(8,128)(2,1)S(1)} all-to-all(bf16[16,64,256]{2,1,0:T(8,128)(2,1)S(1)} %bitcast.86), channel_id=1, replica_groups=mesh['sg'=4,'sr'=4,'my'=8,'mx'=4] {'sg','sr'}, dimensions={0} | all-to-all | bytes 1048576 | tf_op jit(solution)/shard_map/all_to_all | solution.py:62
  172.6 0.1 reduce_sum.51
  172.7 20.0 %all_to_all.16 = bf16[16,64,256]{2,1,0:T(8,128)(2,1)S(1)} all-to-all(bf16[16,64,256]{2,1,0:T(8,128)(2,1)S(1)} %broadcast_in_dim.5), channel_id=1, replica_groups=mesh['sg'=4,'sr'=4,'my'=8,'mx'=4] {'sg','sr'}, dimensions={0} | all-to-all | bytes 1048576 | tf_op jit(solution)/shard_map/all_to_all | solution.py:65
  192.7 0.0 copy-start.1
  192.7 0.9 reshape_reshape.7
  193.6 10.4 %reduce-scatter.2.cloned.1.call-done = bf16[1,4,2,256,128]{4,3,2,1,0:T(8,128)(2,1)} async-done(((bf16[8,4,2,256,128]{4,3,2,1,0:T(8,128)(2,1)}), bf16[1,4,2,256,128]{4,3,2,1,0:T(8,128)(2,1)}) %reduce-scatter.2.cloned.1.call-update) | async-done | bytes 524304 | tf_op jit(solution)/shard_map/reduce_scatter | solution.py:47
  204.1 1.2 copy.20
  205.3 13.6 %all_to_all.17 = bf16[4,2,256,128]{2,3,1,0:T(8,128)(2,1)S(1)} all-to-all(bf16[4,2,256,128]{2,3,1,0:T(8,128)(2,1)S(1)} %copy.20), channel_id=1, replica_groups=mesh['sg'=4,'sr'=4,'my'=8,'mx'=4] {'mx'}, dimensions={0} | all-to-all | bytes 1048576 | tf_op jit(solution)/shard_map/all_to_all | solution.py:49
  218.9 0.1 convert_reduce_fusion
  219.0 0.0 copy-done.1
  219.0 0.0 copy-done.2
  219.0 2.3 collective-permute-start.4
  221.3 0.0 collective-permute-start.3
  221.3 1.9 collective-permute-done.4
  223.2 3.0 %collective-permute-done.3 = bf16[1,128,256]{2,1,0:T(8,128)(2,1)S(1)} collective-permute-done((bf16[1,128,256]{2,1,0:T(8,128)(2,1)S(1)}, bf16[1,128,256]{2,1,0:T(8,128)(2,1)S(1)}, u32[]{:S(2)}, u32[]{:S(2)}) %collective-permute-start.3) | collective-permute-done | bytes 65568 | tf_op jit(solution)/shard_map/ppermute | solution.py:16
  226.2 0.6 copy.32
  226.8 0.6 copy.33
  (11 shorter events, 0.2 us)
Async XLA Ops:
  7.2 15.5 %copy-start.3 = (s32[1,2,2,2]{3,2,1,0:T(2,128)S(1)}, s32[1,2,2,2]{3,2,1,0:T(2,128)}, u32[]{:S(2)}) copy-start(s32[1,2,2,2]{3,2,1,0:T(2,128)} %param.9) | copy-start | bytes 100
  7.2 96.7 %all-gather.2.cloned.1.call-start = ((), (), s32[]{:S(2)}) async-start(), calls=%async_computation.4 | async-start | bytes 7077888 | tf_op jit(solution)/shard_map/all_gather | solution.py:80
  22.6 181.5 %reduce-scatter.2.cloned.1.call-start = ((), (), s32[]{:S(2)}) async-start(), calls=%async_computation.5 | async-start | bytes 4718592 | tf_op jit(solution)/shard_map/reduce_scatter | solution.py:47
  103.9 2.2 slice-start
  103.9 2.9 %copy-start = (bf16[8192,128]{1,0:T(8,128)(2,1)S(1)}, bf16[8192,128]{1,0:T(8,128)(2,1)}, u32[]{:S(2)}) copy-start(bf16[8192,128]{1,0:T(8,128)(2,1)} %get-tuple-element.54) | copy-start | bytes 6291460
  108.1 12.3 %collective-permute-start.2 = (bf16[256,256]{1,0:T(8,128)(2,1)S(1)}, bf16[256,256]{1,0:T(8,128)(2,1)S(1)}, u32[]{:S(2)}, u32[]{:S(2)}) collective-permute-start(bf16[256,256]{1,0:T(8,128)(2,1)S(1)} %get-tuple-element.39), channel_id=1, source_target_pairs={{384,0},{385,1},{386,2},{387,3},{388,4},{389,5},{390,6},{391,7},{3... | collective-permute-start | bytes 393224 | tf_op jit(solution)/shard_map/ppermute | solution.py:110
  109.4 11.0 %collective-permute-start.1 = (bf16[256,256]{1,0:T(8,128)(2,1)S(1)}, bf16[256,256]{1,0:T(8,128)(2,1)S(1)}, u32[]{:S(2)}, u32[]{:S(2)}) collective-permute-start(bf16[256,256]{1,0:T(8,128)(2,1)S(1)} %get-tuple-element.39), channel_id=1, source_target_pairs={{384,128},{385,129},{386,130},{387,131},{388,132},{389,133},{390,1... | collective-permute-start | bytes 393224 | tf_op jit(solution)/shard_map/ppermute | solution.py:110
  110.1 10.3 %collective-permute-start = (bf16[256,256]{1,0:T(8,128)(2,1)S(1)}, bf16[256,256]{1,0:T(8,128)(2,1)S(1)}, u32[]{:S(2)}, u32[]{:S(2)}) collective-permute-start(bf16[256,256]{1,0:T(8,128)(2,1)S(1)} %get-tuple-element.39), channel_id=1, source_target_pairs={{384,256},{385,257},{386,258},{387,259},{388,260},{389,261},{390,2... | collective-permute-start | bytes 393224 | tf_op jit(solution)/shard_map/ppermute | solution.py:110
  192.7 26.3 %copy-start.1 = (bf16[1,2,128,256]{3,2,1,0:T(8,128)(2,1)S(1)}, bf16[1,2,128,256]{3,2,1,0:T(8,128)(2,1)}, u32[]{:S(2)}) copy-start(bf16[1,2,128,256]{3,2,1,0:T(8,128)(2,1)} %param.6) | copy-start | bytes 393220
  192.7 26.3 %copy-start.2 = (bf16[1,128,256]{2,1,0:T(8,128)(2,1)S(1)}, bf16[1,128,256]{2,1,0:T(8,128)(2,1)}, u32[]{:S(2)}) copy-start(bf16[1,128,256]{2,1,0:T(8,128)(2,1)} %param.7) | copy-start | bytes 196612
  219.0 4.2 %collective-permute-start.4 = (bf16[1,128,256]{2,1,0:T(8,128)(2,1)S(1)}, bf16[1,128,256]{2,1,0:T(8,128)(2,1)S(1)}, u32[]{:S(2)}, u32[]{:S(2)}) collective-permute-start(bf16[1,128,256]{2,1,0:T(8,128)(2,1)S(1)} %get-tuple-element.56), channel_id=1, source_target_pairs={{0,480},{32,0},{64,32},{96,64},{128,96},{160,128},{192,160},{224,1... | collective-permute-start | bytes 196616 | tf_op jit(solution)/shard_map/ppermute | solution.py:16
  221.3 4.9 %collective-permute-start.3 = (bf16[1,128,256]{2,1,0:T(8,128)(2,1)S(1)}, bf16[1,128,256]{2,1,0:T(8,128)(2,1)S(1)}, u32[]{:S(2)}, u32[]{:S(2)}) collective-permute-start(bf16[1,128,256]{2,1,0:T(8,128)(2,1)S(1)} %get-tuple-element.57), channel_id=1, source_target_pairs={{0,32},{32,64},{64,96},{96,128},{128,160},{160,192},{192,224},{224... | collective-permute-start | bytes 196616 | tf_op jit(solution)/shard_map/ppermute | solution.py:16
Sparse Core Ops, SparseCore 0:
  22.7 81.0 all-gather.1
  148.7 55.3 reduce-scatter.1
where the time goes:
time: 235 us; the launch traced here: 234 us
  waiting for transfers between devices  99.2 us (42%)
  blocking collectives  81 us (34%)
  local copies, waits for them, and re-layouts  17.2 us (7%)
  between operations  14.3 us (6%)
  matrix products  11.3 us (5%)
  other arithmetic  6.31 us (3%)
  starting transfers between devices  4.98 us (2%)
    all_gather x1, waiting for transfers between devices, per_device(): gathered = lax.all_gather(gathered, stage, axis=2, tiled=True)  77.2 us
    all_to_all x1, blocking collectives, segment_sum(): moved = lax.all_to_all(parts, axis, 0, 0, tiled=True)  21.9 us
    all_to_all x1, blocking collectives, segment_sum(): return lax.all_to_all(spread, axis, 0, 0, tiled=True).reshape(contrib.shape)  20 us
    all_gather x1, blocking collectives, per_device(): gathered = lax.all_gather(gathered, stage, axis=2, tiled=True)  14.4 us
    all_to_all x1, blocking collectives, head_sum(): moved = lax.all_to_all(partial, axis[1], 0, 0, tiled=True)  13.6 us
    all_gather x1, blocking collectives, per_device(): lax.all_gather(piece, 'sr', axis=0, tiled=True)  11.1 us
    reduce_scatter x1, waiting for transfers between devices, head_sum(): lax.psum_scatter(parts, axis[0], scatter_dimension=0, tiled=True)[0]  10.4 us
    ppermute x3, waiting for transfers between devices, per_device(): arrived = lax.ppermute(encoded, 'sg', [(last_group, target)])  6.71 us
  transfers between devices with their start and end apart: 7, of which 5 were waited for; matrix products, arithmetic and copies ran while one was open for 4% of the time, Pallas kernels for 0%

commit v1 on v0

--- a/solution.py
+++ b/solution.py
@@ -77,7 +77,9 @@
     local_carry = carry[0]
     gathered = jnp.concatenate([local_rows, local_carry[None]], axis=0)
     for stage in stages:
-        gathered = lax.all_gather(gathered, stage, axis=2, tiled=True)
+        gathered = jnp.concatenate(
+            lax.all_to_all(jnp.stack([gathered] * lax.axis_size(stage)), stage, 0, 0), axis=2
+        )
     full_rows, full_carry = (gathered[:2], gathered[2])
     tokens = local_rows.shape[1]
     width = full_rows.shape[2]

time: 235 us -> 331 us (1.41)
  waiting for transfers between devices: 99.2 us -> 161 us
  local copies, waits for them, and re-layouts: 17.2 us -> 41.1 us
  starting transfers between devices: 4.98 us -> 12.4 us
    all_to_all x0 -> x1, waiting for transfers between devices: none -> 127 us  [per_device(): lax.all_to_all(jnp.stack([gathered] * lax.axis_size(stage)), stage, 0, 0)]
    all_gather x1 -> x0, waiting for transfers between devices: 77.2 us -> none  [per_device(): gathered = lax.all_gather(gathered, stage, axis=2, tiled=True)]
    all_to_all x0 -> x1, blocking collectives: none -> 16.4 us  [per_device(): lax.all_to_all(jnp.stack([gathered] * lax.axis_size(stage)), stage, 0, 0)]
    all_gather x1 -> x0, blocking collectives: 14.4 us -> none  [per_device(): gathered = lax.all_gather(gathered, stage, axis=2, tiled=True)]
    another operation x1 -> x5, local copies, waits for them, and re-layouts: 0.01 us -> 10.2 us
    all_to_all x0 -> x2, local copies, waits for them, and re-layouts: none -> 8.98 us  [per_device(): lax.all_to_all(jnp.stack([gathered] * lax.axis_size(stage)), stage, 0, 0)]
    reduce_scatter x1, waiting for transfers between devices: 10.4 us -> 18.9 us  [head_sum(): lax.psum_scatter(parts, axis[0], scatter_dimension=0, tiled=True)[0]]
    all_to_all x0 -> x1, starting transfers between devices: none -> 7.45 us  [per_device(): lax.all_to_all(jnp.stack([gathered] * lax.axis_size(stage)), stage, 0, 0)]
  transfers between devices with their start and end apart: 7 -> 7, of which waited for: 5 -> 5; matrix products, arithmetic and copies ran while one was open for 4% -> 3% of each run, Pallas kernels for 0% -> 0%
where the time goes in v1:
time: 331 us; the launch traced here: 330 us
  waiting for transfers between devices  161 us (49%)
  blocking collectives  81.2 us (25%)
  local copies, waits for them, and re-layouts  41.1 us (12%)
  between operations  14.3 us (4%)
  matrix products  13.5 us (4%)
  starting transfers between devices  12.4 us (4%)
  other arithmetic  6.31 us (2%)
    all_to_all x1, waiting for transfers between devices, per_device(): lax.all_to_all(jnp.stack([gathered] * lax.axis_size(stage)), stage, 0, 0)  127 us
    all_to_all x1, blocking collectives, segment_sum(): moved = lax.all_to_all(parts, axis, 0, 0, tiled=True)  21.1 us
    all_to_all x1, blocking collectives, segment_sum(): return lax.all_to_all(spread, axis, 0, 0, tiled=True).reshape(contrib.shape)  20 us
    reduce_scatter x1, waiting for transfers between devices, head_sum(): lax.psum_scatter(parts, axis[0], scatter_dimension=0, tiled=True)[0]  18.9 us
    all_to_all x1, blocking collectives, per_device(): lax.all_to_all(jnp.stack([gathered] * lax.axis_size(stage)), stage, 0, 0)  16.4 us
    all_to_all x1, blocking collectives, head_sum(): moved = lax.all_to_all(partial, axis[1], 0, 0, tiled=True)  13.6 us
    ppermute x3, waiting for transfers between devices, per_device(): arrived = lax.ppermute(encoded, 'sg', [(last_group, target)])  10.5 us
    all_gather x1, blocking collectives, per_device(): lax.all_gather(piece, 'sr', axis=0, tiled=True)  10 us
  transfers between devices with their start and end apart: 7, of which 5 were waited for; matrix products, arithmetic and copies ran while one was open for 3% of the time, Pallas kernels for 0%

profile of v1, /device:TPU:24, one launch (start us, length us, event | category | flops | bytes accessed | tf_op | source)
XLA Modules:
  0.0 329.7 jit_solution(4014596026994226884)
XLA Ops:
  7.2 1.0 pad_maximum_fusion.2
  8.1 0.1 stack.19
  8.2 16.4 %all_to_all.25 = bf16[4,3,128,256]{3,2,1,0:T(8,128)(2,1)S(1)} all-to-all(bf16[4,3,128,256]{3,2,1,0:T(8,128)(2,1)S(1)} %stack.19), channel_id=1, replica_groups=mesh['sg'=4,'sr'=4,'my'=8,'mx'=4] {'mx'}, dimensions={0} | all-to-all | bytes 1572864 | tf_op jit(solution)/shard_map/all_to_all | solution.py:81
  24.6 0.4 copy.22
  25.0 0.3 copy.23
  25.3 3.5 %stack.20 = bf16[8,3,128,1024]{3,2,1,0:T(8,128)(2,1)} broadcast(bf16[3,128,1024]{2,1,0:T(8,128)(2,1)S(1)} %copy.23), dimensions={1,2,3} | broadcast | bytes 7077888 | tf_op jit(solution)/shard_map/stack | solution.py:81
  28.8 7.5 %all-to-all-start.1 = ((bf16[8,3,128,1024]{3,2,1,0:T(8,128)(2,1)}), bf16[8,3,128,1024]{3,2,1,0:T(8,128)(2,1)}, u32[]{:S(2)}, u32[]{:S(2)}) async-start(bf16[8,3,128,1024]{3,2,1,0:T(8,128)(2,1)} %stack.20), calls=%async_computation.1 | async-start | bytes 12582912 | tf_op jit(solution)/shard_map/all_to_all | solution.py:81
  36.2 0.0 reduce-scatter.2.cloned.1.call-start
  36.2 0.0 copy-done.3
  36.2 0.1 reshape.155
  36.3 0.1 reshape.163
  36.4 3.8 %slice_bitcast_fusion = (bf16[8192,128]{1,0:T(8,128)(2,1)}, bf16[8192,128]{1,0:T(8,128)(2,1)S(1)}) fusion(bf16[1,2,8192,128]{3,2,1,0:T(8,128)(2,1)} %param.8), kind=kLoop, calls=%fused_computation.13 | loop fusion | bytes 8388608 | tf_op jit(solution)/shard_map/squeeze | solution.py:88
  40.3 126.7 %all-to-all-done.1 = bf16[8,3,128,1024]{3,2,1,0:T(8,128)(2,1)} async-done(((bf16[8,3,128,1024]{3,2,1,0:T(8,128)(2,1)}), bf16[8,3,128,1024]{3,2,1,0:T(8,128)(2,1)}, u32[]{:S(2)}, u32[]{:S(2)}) %all-to-all-start.1) | async-done | bytes 6291488 | tf_op jit(solution)/shard_map/all_to_all | solution.py:81
  166.9 8.6 %copy.24 = bf16[8,3,128,1024]{2,3,0,1:T(8,128)(2,1)} copy(bf16[8,3,128,1024]{3,2,1,0:T(8,128)(2,1)} %all-to-all-done.1) | data formatting | bytes 12582912 | tf_op jit(solution)/shard_map/all_to_all | solution.py:81
  175.6 3.0 slice.80
  178.6 4.6 %slice.76 = bf16[2,128,8,1024]{1,3,2,0:T(8,128)(2,1)} slice(bf16[3,128,8,1024]{1,3,2,0:T(8,128)(2,1)} %bitcast.86), slice={[0:2], [0:128], [0:8], [0:1024]} | slice | bytes 8388608 | tf_op jit(solution)/shard_map/slice | solution.py:83
  183.2 9.8 %conditional.1 = (bf16[256,256]{1,0:T(8,128)(2,1)S(1)}, bf16[2,64,128]{2,1,0:T(8,128)(2,1)S(1)}, bf16[2,64,128]{2,1,0:T(8,128)(2,1)S(1)}) conditional(s32[]{:T(128)} %convert_element_type.64, (bf16[2,128,8192]{1,2,0:T(8,128)(2,1)}, bf16[8192,128]{1,0:T(8,128)(2,1)S(1)}) %tuple.45, (bf16[2,128,8192]{1,2,0:T(8,128)(2,1)}, ...), branch_computations={%region_0.0_spmd, %region_1.0_spmd} | conditional | flops 1074069504 | bytes 38469688 | solution.py:107
  183.2 6.3 %copy.25 = bf16[2,128,8192]{2,1,0:T(8,128)(2,1)} copy(bf16[2,128,8192]{1,2,0:T(8,128)(2,1)} %get-tuple-element.55) | data formatting | bytes 8388608 | tf_op jit(solution)/shard_map
  189.5 3.4 %convolution_convert_fusion = bf16[256,128]{1,0:T(8,128)(2,1)S(1)} fusion(bf16[256,8192]{1,0:T(8,128)(2,1)} %bitcast.87, bf16[8192,128]{1,0:T(8,128)(2,1)S(1)} %get-tuple-element.26), kind=kOutput, calls=%fused_computation.2 | convolution fusion | flops 536903680 | bytes 6356992 | tf_op jit(solution)/shard_map/cond/branch_0_fun/dot_general | solution.py:102
  193.0 1.3 collective-permute-start.2
  194.3 0.7 collective-permute-start.1
  194.9 0.7 collective-permute-start
  195.6 3.0 convolution_convert_fusion.5
  198.6 10.5 %collective-permute-done.2 = bf16[256,256]{1,0:T(8,128)(2,1)S(1)} collective-permute-done((bf16[256,256]{1,0:T(8,128)(2,1)S(1)}, bf16[256,256]{1,0:T(8,128)(2,1)S(1)}, u32[]{:S(2)}, u32[]{:S(2)}) %collective-permute-start.2) | collective-permute-done | bytes 131104 | tf_op jit(solution)/shard_map/ppermute | solution.py:112
  209.1 0.0 collective-permute-done.1
  209.1 0.0 collective-permute-done
  209.1 10.0 %all_gather.3 = bf16[1024,256]{1,0:T(8,128)(2,1)S(1)} all-gather(bf16[256,256]{1,0:T(8,128)(2,1)S(1)} %select_select_fusion), channel_id=1, replica_groups=mesh['sg'=4,'sr'=4,'my'=8,'mx'=4] {'sr'}, dimensions={0}, use_global_device_ids=true | all-gather | bytes 655360 | tf_op jit(solution)/shard_map/all_gather | solution.py:114
  219.2 0.6 gather_fusion.1
  219.7 0.6 gather_fusion
  220.3 0.2 convolution_multiply_fusion.2
  220.5 0.2 fusion.31
  220.7 0.3 convolution_convert_fusion.6
  221.0 0.2 convolution_multiply_fusion.1
  221.2 0.4 fusion.30
  221.5 0.3 multiply_reduce_fusion
  221.8 0.3 fusion.10
  222.1 2.3 fusion.3
  224.5 2.5 copy.35
  226.9 2.3 fusion.2
  229.2 2.5 copy.34
  231.7 4.5 %maximum_bitcast_fusion = bf16[8,4,2,256,128]{4,3,2,1,0:T(8,128)(2,1)} fusion(bf16[1,8,4,256,128]{4,3,0,2,1:T(8,128)(2,1)} %bitcast.88, bf16[1,8,4,256,128]{4,3,0,2,1:T(8,128)(2,1)} %bitcast.89), kind=kLoop, calls=%fused_computation.12 | loop fusion | flops 2097152 | bytes 8388608 | tf_op jit(solution)/shard_map/transpose | solution.py:44
  236.2 0.0 reduce-scatter.2.cloned.1.call-update
  236.3 0.1 copy.29
  236.3 0.3 fusion.21
  236.7 0.4 convolution_multiply_fusion
  237.1 0.1 reshape.151
  237.2 0.5 copy.30
  237.7 0.5 fusion.5
  238.2 0.1 copy.31
  238.3 21.1 %all_to_all.26 = bf16[16,64,256]{2,1,0:T(8,128)(2,1)S(1)} all-to-all(bf16[16,64,256]{2,1,0:T(8,128)(2,1)S(1)} %bitcast.94), channel_id=1, replica_groups=mesh['sg'=4,'sr'=4,'my'=8,'mx'=4] {'sg','sr'}, dimensions={0} | all-to-all | bytes 1048576 | tf_op jit(solution)/shard_map/all_to_all | solution.py:62
  259.4 0.1 reduce_sum.51
  259.6 20.0 %all_to_all.27 = bf16[16,64,256]{2,1,0:T(8,128)(2,1)S(1)} all-to-all(bf16[16,64,256]{2,1,0:T(8,128)(2,1)S(1)} %broadcast_in_dim.5), channel_id=1, replica_groups=mesh['sg'=4,'sr'=4,'my'=8,'mx'=4] {'sg','sr'}, dimensions={0} | all-to-all | bytes 1048576 | tf_op jit(solution)/shard_map/all_to_all | solution.py:65
  279.6 0.9 reshape_reshape.7
  280.5 18.9 %reduce-scatter.2.cloned.1.call-done = bf16[1,4,2,256,128]{4,3,2,1,0:T(8,128)(2,1)} async-done(((bf16[8,4,2,256,128]{4,3,2,1,0:T(8,128)(2,1)}), bf16[1,4,2,256,128]{4,3,2,1,0:T(8,128)(2,1)}) %reduce-scatter.2.cloned.1.call-update) | async-done | bytes 524304 | tf_op jit(solution)/shard_map/reduce_scatter | solution.py:47
  299.4 1.2 copy.32
  300.7 13.6 %all_to_all.28 = bf16[4,2,256,128]{2,3,1,0:T(8,128)(2,1)S(1)} all-to-all(bf16[4,2,256,128]{2,3,1,0:T(8,128)(2,1)S(1)} %copy.32), channel_id=1, replica_groups=mesh['sg'=4,'sr'=4,'my'=8,'mx'=4] {'mx'}, dimensions={0} | all-to-all | bytes 1048576 | tf_op jit(solution)/shard_map/all_to_all | solution.py:49
  314.3 0.1 convert_reduce_fusion
  314.3 0.0 copy-done.1
  314.4 2.3 collective-permute-start.4
  316.7 0.0 collective-permute-start.3
  316.7 1.9 collective-permute-done.4
  318.6 3.0 collective-permute-done.3
  321.6 0.6 copy.44
  322.2 0.6 copy.45
  (14 shorter events, 0.2 us)
Async XLA Ops:
  28.8 7.5 %copy-start.3 = (s32[1,2,2,2]{3,2,1,0:T(2,128)S(1)}, s32[1,2,2,2]{3,2,1,0:T(2,128)}, u32[]{:S(2)}) copy-start(s32[1,2,2,2]{3,2,1,0:T(2,128)} %param.9) | copy-start | bytes 100
  28.8 138.2 %all-to-all-start.1 = ((bf16[8,3,128,1024]{3,2,1,0:T(8,128)(2,1)}), bf16[8,3,128,1024]{3,2,1,0:T(8,128)(2,1)}, u32[]{:S(2)}, u32[]{:S(2)}) async-start(bf16[8,3,128,1024]{3,2,1,0:T(8,128)(2,1)} %stack.20), calls=%async_computation.1 | async-start | bytes 12582912 | tf_op jit(solution)/shard_map/all_to_all | solution.py:81
  36.2 263.2 %reduce-scatter.2.cloned.1.call-start = ((), (), s32[]{:S(2)}) async-start(), calls=%async_computation.6 | async-start | bytes 4718592 | tf_op jit(solution)/shard_map/reduce_scatter | solution.py:47
  193.0 16.1 %collective-permute-start.2 = (bf16[256,256]{1,0:T(8,128)(2,1)S(1)}, bf16[256,256]{1,0:T(8,128)(2,1)S(1)}, u32[]{:S(2)}, u32[]{:S(2)}) collective-permute-start(bf16[256,256]{1,0:T(8,128)(2,1)S(1)} %get-tuple-element.39), channel_id=1, source_target_pairs={{384,0},{385,1},{386,2},{387,3},{388,4},{389,5},{390,6},{391,7},{3... | collective-permute-start | bytes 393224 | tf_op jit(solution)/shard_map/ppermute | solution.py:112
  194.3 14.8 %collective-permute-start.1 = (bf16[256,256]{1,0:T(8,128)(2,1)S(1)}, bf16[256,256]{1,0:T(8,128)(2,1)S(1)}, u32[]{:S(2)}, u32[]{:S(2)}) collective-permute-start(bf16[256,256]{1,0:T(8,128)(2,1)S(1)} %get-tuple-element.39), channel_id=1, source_target_pairs={{384,128},{385,129},{386,130},{387,131},{388,132},{389,133},{390,1... | collective-permute-start | bytes 393224 | tf_op jit(solution)/shard_map/ppermute | solution.py:112
  194.9 14.2 %collective-permute-start = (bf16[256,256]{1,0:T(8,128)(2,1)S(1)}, bf16[256,256]{1,0:T(8,128)(2,1)S(1)}, u32[]{:S(2)}, u32[]{:S(2)}) collective-permute-start(bf16[256,256]{1,0:T(8,128)(2,1)S(1)} %get-tuple-element.39), channel_id=1, source_target_pairs={{384,256},{385,257},{386,258},{387,259},{388,260},{389,261},{390,2... | collective-permute-start | bytes 393224 | tf_op jit(solution)/shard_map/ppermute | solution.py:112
  279.6 34.8 %copy-start.1 = (bf16[1,2,128,256]{3,2,1,0:T(8,128)(2,1)S(1)}, bf16[1,2,128,256]{3,2,1,0:T(8,128)(2,1)}, u32[]{:S(2)}) copy-start(bf16[1,2,128,256]{3,2,1,0:T(8,128)(2,1)} %param.6) | copy-start | bytes 393220
  279.6 34.8 %copy-start.2 = (bf16[1,128,256]{2,1,0:T(8,128)(2,1)S(1)}, bf16[1,128,256]{2,1,0:T(8,128)(2,1)}, u32[]{:S(2)}) copy-start(bf16[1,128,256]{2,1,0:T(8,128)(2,1)} %param.7) | copy-start | bytes 196612
  314.4 4.2 %collective-permute-start.4 = (bf16[1,128,256]{2,1,0:T(8,128)(2,1)S(1)}, bf16[1,128,256]{2,1,0:T(8,128)(2,1)S(1)}, u32[]{:S(2)}, u32[]{:S(2)}) collective-permute-start(bf16[1,128,256]{2,1,0:T(8,128)(2,1)S(1)} %get-tuple-element.64), channel_id=1, source_target_pairs={{0,480},{32,0},{64,32},{96,64},{128,96},{160,128},{192,160},{224,1... | collective-permute-start | bytes 196616 | tf_op jit(solution)/shard_map/ppermute | solution.py:16
  316.7 4.9 %collective-permute-start.3 = (bf16[1,128,256]{2,1,0:T(8,128)(2,1)S(1)}, bf16[1,128,256]{2,1,0:T(8,128)(2,1)S(1)}, u32[]{:S(2)}, u32[]{:S(2)}) collective-permute-start(bf16[1,128,256]{2,1,0:T(8,128)(2,1)S(1)} %get-tuple-element.65), channel_id=1, source_target_pairs={{0,32},{32,64},{64,96},{96,128},{128,160},{160,192},{192,224},{224... | collective-permute-start | bytes 196616 | tf_op jit(solution)/shard_map/ppermute | solution.py:16
Sparse Core Ops, SparseCore 0:
  236.4 63.0 reduce-scatter.1
